TPU v7x, 32 devices: a whole 2x2x4 slice. The times are simulated.
32 devices in a mesh: brick: 4 (over z), batch: 8 (over y, x, core).
Axes of the slice: x: 2, y: 2, z: 4, core: 2. Of those that a mesh axis runs over, the one named last changes fastest.
Arguments:
- coarse: bfloat16 [8, 4, 4, 8, 1024], P('batch', 'brick'), may hold values from -6 to 6
- coarse_mask: int32 [8, 4, 256], P('batch', 'brick'), may hold values 0 or 1
- skip: bfloat16 [8, 4, 8, 16, 1024], P('batch', 'brick'), may hold values from -6 to 6
- fine_mask: int32 [8, 4, 2048], P('batch', 'brick'), may hold values 0 or 1
- up_weight: bfloat16 [27, 64, 128], replicated, may hold values from -0.25 to 0.25
- fine_grad: bfloat16 [8, 4, 8, 16, 1024], P('batch', 'brick'), may hold values from -6 to 6
Outputs:
- fine_out: bfloat16 [8, 4, 8, 16, 1024], P('batch', 'brick')
- coarse_grad: bfloat16 [8, 4, 4, 8, 1024], P('batch', 'brick')
- weight_grad: float32 [27, 64, 128], replicated
All inputs are finite; a program needn't handle non-finite values. No bound on the sum of `coarse_mask` or of `fine_mask` on one device may be relied on, other than what follows from the above.
Results may differ from a plain program's by a relative error of at most 0.0035.
Values may be sent and summed in bfloat16 or wider, within the bound.
No kernel may reach another device: no remote copies, remote signals or barrier semaphores. Data moves between devices by JAX's collectives and lax.ppermute only.
A program may use at most 64 MiB of HBM per device.

v0:
```python
import math
import jax
import jax.numpy as jnp
from jax import lax
from jax.sharding import PartitionSpec as P

EVEN_TAPS = ((1, 0),)
ODD_TAPS = ((2, 0), (0, 1))
DIRECTIONS = ((1, 0, 0), (0, 1, 0), (0, 0, 1), (1, 1, 0), (1, 0, 1), (0, 1, 1), (1, 1, 1))
STRIDES = (4, 2, 1)


def from_behind(shard, axis, by):
    size = lax.axis_size(axis)
    pairs = [(i, i + by) for i in range(size) if 0 <= i + by < size]
    return lax.ppermute(shard, axis, pairs)


def tap_pairs(parity):
    if parity == 0:
        return EVEN_TAPS
    return ODD_TAPS


def spread(padded, weight):
    counts = (padded.shape[0] - 1, padded.shape[1] - 1, padded.shape[2] - 1)
    outputs = weight.shape[1]
    parts = []
    for parity_x in range(2):
        for parity_y in range(2):
            for parity_z in range(2):
                total = jnp.zeros(counts + (outputs,), jnp.float32)
                for tap_x, start_x in tap_pairs(parity_x):
                    for tap_y, start_y in tap_pairs(parity_y):
                        for tap_z, start_z in tap_pairs(parity_z):
                            window = padded[
                                start_x : start_x + counts[0],
                                start_y : start_y + counts[1],
                                start_z : start_z + counts[2],
                            ]
                            total = total + jnp.einsum(
                                "abci,oi->abco",
                                window,
                                weight[9 * tap_x + 3 * tap_y + tap_z],
                                preferred_element_type=jnp.float32,
                            )
                parts.append(total)
    stacked = jnp.stack(parts).reshape((2, 2, 2) + counts + (outputs,))
    return stacked.transpose(3, 0, 4, 1, 5, 2, 6).reshape(
        2 * counts[0], 2 * counts[1], 2 * counts[2], outputs
    )


def pick(field, tap, count, axis):
    return lax.slice_in_dim(field, tap, tap + 2 * count - 1, 2, axis)


def adjoint(widened, masked, weight):
    counts = masked.shape[:3]
    back = jnp.zeros(masked.shape, jnp.float32)
    grads = []
    for tap_x in range(3):
        along_x = pick(widened, tap_x, counts[0], 0)
        for tap_y in range(3):
            along_y = pick(along_x, tap_y, counts[1], 1)
            for tap_z in range(3):
                chosen = pick(along_y, tap_z, counts[2], 2)
                index = 9 * tap_x + 3 * tap_y + tap_z
                back = back + jnp.einsum(
                    "abco,oi->abci", chosen, weight[index], preferred_element_type=jnp.float32
                )
                grads.append(
                    jnp.einsum("abco,abci->oi", chosen, masked, preferred_element_type=jnp.float32)
                )
    return (back, jnp.stack(grads))


def offset(direction):
    return 4 * direction[0] + 2 * direction[1] + direction[2]


def allowed(direction, grid_y, grid_z, side):
    result = grid_y >= 0
    if direction[1]:
        result = result & (grid_y == side)
    if direction[2]:
        result = result & (grid_z == side)
    return result


def flatten(piece):
    return piece.reshape(piece.shape[0], -1)


def segment_index(other, axis, edge):
    if other < axis:
        return slice(1, None)
    if other > axis:
        return slice(None)
    return edge


def unit_of(axis):
    return tuple((1 if other == axis else 0 for other in range(3)))


def body(coarse, coarse_mask, skip, fine_mask, up_weight, fine_grad):
    rank = lax.axis_index("brick")
    grid_y = rank // 2 % 2
    grid_z = rank % 2
    size_x, size_y, merged = coarse.shape[2:]
    channels_out = up_weight.shape[1]
    channels_in = up_weight.shape[2]
    size_z = merged // channels_in
    fine_x, fine_y, fine_merged = skip.shape[2:]
    fine_z = fine_merged // channels_out
    coarse_keep = coarse_mask.reshape(size_x, size_y, size_z, 1).astype(jnp.bfloat16)
    masked = coarse.reshape(size_x, size_y, size_z, channels_in) * coarse_keep
    extended = spread(jnp.pad(masked, ((1, 1), (1, 1), (1, 1), (0, 0))), up_weight)[1:, 1:, 1:]
    for axis in range(3):
        source = tuple((segment_index(other, axis, slice(0, 1)) for other in range(3)))
        piece = extended[source]
        got = from_behind(flatten(piece).astype(jnp.bfloat16), "brick", -STRIDES[axis]).astype(
            jnp.float32
        )
        got = jnp.where(allowed(unit_of(axis), grid_y, grid_z, 0), got, 0.0).reshape(piece.shape)
        target = tuple((segment_index(other, axis, slice(-1, None)) for other in range(3)))
        extended = extended.at[target].add(got)
    up = extended[1:, 1:, 1:]
    fine_keep = fine_mask.reshape(fine_x, fine_y, fine_z, 1)
    fine = fine_keep.astype(jnp.float32) * (
        skip.reshape(fine_x, fine_y, fine_z, channels_out).astype(jnp.float32) + up
    )
    fine_out = fine.astype(jnp.bfloat16).reshape(skip.shape)
    cotangent = fine_grad.reshape(fine_x, fine_y, fine_z, channels_out) * fine_keep.astype(
        jnp.bfloat16
    )
    widened = jnp.pad(cotangent, ((1, 0), (1, 0), (1, 0), (0, 0)))
    for direction in DIRECTIONS:
        source = tuple((slice(-1, None) if flag else slice(None) for flag in direction))
        piece = cotangent[source]
        got = from_behind(flatten(piece), "brick", offset(direction))
        got = jnp.where(allowed(direction, grid_y, grid_z, 1), got, 0.0).reshape(piece.shape)
        target = tuple((slice(0, 1) if flag else slice(1, None) for flag in direction))
        widened = widened.at[target].set(got)
    back, grads = adjoint(widened, masked, up_weight)
    coarse_grad = (
        (back * coarse_keep.astype(jnp.float32)).astype(jnp.bfloat16).reshape(coarse.shape)
    )
    summed = lax.psum(grads, ("brick", "batch"))
    scale = 1.0 / math.sqrt(
        lax.axis_size("brick") * lax.axis_size("batch") * size_x * size_y * size_z
    )
    return (fine_out, coarse_grad, summed * scale)


def solution(mesh):
    in_specs = (
        P("batch", "brick", None, None, None),
        P("batch", "brick", None),
        P("batch", "brick", None, None, None),
        P("batch", "brick", None),
        P(),
        P("batch", "brick", None, None, None),
    )
    out_specs = (P("batch", "brick", None, None, None), P("batch", "brick", None, None, None), P())
    return jax.shard_map(body, mesh=mesh, in_specs=in_specs, out_specs=out_specs, check_vma=False)
```

profile of v0, /device:TPU:0, one launch (start us, length us, event | category | flops | bytes accessed | tf_op | source)
XLA Modules:
  0.0 260.1 jit_solution(2375744965565836065)
XLA Ops:
  11.3 5.9 %collective-permute-start.4 = (bf16[8,1024]{1,0:T(8,128)(2,1)S(1)}, bf16[8,1024]{1,0:T(8,128)(2,1)S(1)}, u32[]{:S(2)}, u32[]{:S(2)}) collective-permute-start(bf16[8,1024]{1,0:T(8,128)(2,1)S(1)} %reshape.526), channel_id=1, source_target_pairs={{0,16},{8,24},{1,17},{9,25},{2,18},{10,26},{3,19},{11,27},{4,20},{... | collective-permute-start | bytes 49160 | tf_op jit(solution)/shard_map/ppermute | solution.py:16
  17.6 3.5 %collective-permute-start.5 = (bf16[8,1024]{1,0:T(8,128)(2,1)S(1)}, bf16[8,1024]{1,0:T(8,128)(2,1)S(1)}, u32[]{:S(2)}, u32[]{:S(2)}) collective-permute-start(bf16[8,1024]{1,0:T(8,128)(2,1)S(1)} %reshape.528), channel_id=1, source_target_pairs={{0,8},{8,16},{16,24},{1,9},{9,17},{17,25},{2,10},{10,18},{18,26},{... | collective-permute-start | bytes 49160 | tf_op jit(solution)/shard_map/ppermute | solution.py:16
  31.6 2.0 copy.82
  33.7 2.4 reshape.518
  39.8 2.2 reshape.539
  63.2 2.4 fusion.190
  65.6 2.8 %slice.746 = bf16[4,8,8,64]{3,2,1,0:T(8,128)(2,1)} slice(bf16[4,8,17,64]{3,2,1,0:T(8,128)(2,1)} %get-tuple-element.135), slice={[0:4:1], [0:8:1], [0:15:2], [0:64:1]} | slice | bytes 65536 | tf_op jit(solution)/shard_map/slice | solution.py:55
  68.4 2.8 %slice.747 = bf16[4,8,8,64]{3,2,1,0:T(8,128)(2,1)} slice(bf16[4,8,17,64]{3,2,1,0:T(8,128)(2,1)} %get-tuple-element.135), slice={[0:4:1], [0:8:1], [1:16:2], [0:64:1]} | slice | bytes 65536 | tf_op jit(solution)/shard_map/slice | solution.py:55
  71.1 2.8 %slice.748 = bf16[4,8,8,64]{3,2,1,0:T(8,128)(2,1)} slice(bf16[4,8,17,64]{3,2,1,0:T(8,128)(2,1)} %get-tuple-element.135), slice={[0:4:1], [0:8:1], [2:17:2], [0:64:1]} | slice | bytes 65536 | tf_op jit(solution)/shard_map/slice | solution.py:55
  74.0 2.8 %slice.750 = bf16[4,8,8,64]{3,2,1,0:T(8,128)(2,1)} slice(bf16[4,8,17,64]{3,2,1,0:T(8,128)(2,1)} %get-tuple-element.136), slice={[0:4:1], [0:8:1], [0:15:2], [0:64:1]} | slice | bytes 65536 | tf_op jit(solution)/shard_map/slice | solution.py:55
  76.7 2.7 %slice.751 = bf16[4,8,8,64]{3,2,1,0:T(8,128)(2,1)} slice(bf16[4,8,17,64]{3,2,1,0:T(8,128)(2,1)} %get-tuple-element.136), slice={[0:4:1], [0:8:1], [1:16:2], [0:64:1]} | slice | bytes 65536 | tf_op jit(solution)/shard_map/slice | solution.py:55
  79.5 2.8 %slice.752 = bf16[4,8,8,64]{3,2,1,0:T(8,128)(2,1)} slice(bf16[4,8,17,64]{3,2,1,0:T(8,128)(2,1)} %get-tuple-element.136), slice={[0:4:1], [0:8:1], [2:17:2], [0:64:1]} | slice | bytes 65536 | tf_op jit(solution)/shard_map/slice | solution.py:55
  91.1 1.7 fusion.43
  93.9 1.7 fusion.42
  95.6 1.7 fusion.41
  97.3 1.7 fusion.40
  98.9 1.7 fusion.39
  138.3 1.7 fusion.48
  145.1 4.1 %collective-permute-done.1 = bf16[8,1088]{1,0:T(8,128)(2,1)S(1)} collective-permute-done((bf16[8,1088]{1,0:T(8,128)(2,1)S(1)}, bf16[8,1088]{1,0:T(8,128)(2,1)S(1)}, u32[]{:S(2)}, u32[]{:S(2)}) %collective-permute-start.1) | collective-permute-done | bytes 17440 | tf_op jit(solution)/shard_map/ppermute | solution.py:16
  155.1 2.8 %collective-permute-done.2 = bf16[8,1024]{1,0:T(8,128)(2,1)S(1)} collective-permute-done((bf16[8,1024]{1,0:T(8,128)(2,1)S(1)}, bf16[8,1024]{1,0:T(8,128)(2,1)S(1)}, u32[]{:S(2)}, u32[]{:S(2)}) %collective-permute-start.2) | collective-permute-done | bytes 16416 | tf_op jit(solution)/shard_map/ppermute | solution.py:16
  159.1 3.0 %scatter-add.14 = f32[9,17,17,64]{3,2,1,0:T(8,128)} dynamic-update-slice(f32[9,17,17,64]{3,2,1,0:T(8,128)} %fusion.47, f32[8,16,1,64]{3,2,1,0:T(1,128)S(1)} %slice_add_fusion.3, s32[]{:T(128)} %constant.355.clone.1, s32[]{:T(128)} %constant.355.clone.1, s32[]{:T(128)} %constant.361.clone.1, s32[]{:T(128)} %constant.356.clone.1) | dynamic-update-slice | bytes 65540 | tf_op jit(solution)/shard_map/scatter-add | solution.py:128
  162.1 1.7 fusion.45
  164.9 86.2 %all-reduce.4.cloned.1.call-done = f32[27,64,128]{2,1,0:T(8,128)} async-done(((f32[27,64,128]{2,1,0:T(8,128)}), f32[27,64,128]{2,1,0:T(8,128)}) %all-reduce.4.cloned.1.call-update) | async-done | bytes 884752 | tf_op jit(solution)/shard_map/psum | solution.py:150
  251.1 2.2 broadcast_multiply_fusion
  (248 shorter events, 99.8 us)
Async XLA Ops:
  7.2 18.2 %copy-start.2 = (bf16[27,64,128]{2,1,0:T(8,128)(2,1)S(1)}, bf16[27,64,128]{2,1,0:T(8,128)(2,1)}, u32[]{:S(2)}) copy-start(bf16[27,64,128]{2,1,0:T(8,128)(2,1)} %param.30) | copy-start | bytes 1327108
  7.2 243.9 %all-reduce.4.cloned.1.call-start = ((), (), s32[]{:S(2)}) async-start(), calls=%async_computation | async-start | bytes 1769472 | tf_op jit(solution)/shard_map/psum | solution.py:150
  9.8 17.7 %copy-start.1 = (bf16[8,16,16,64]{3,2,1,0:T(8,128)(2,1)}, bf16[8,16,16,64]{3,2,1,0:T(8,128)(2,1)S(1)}, u32[]{:S(2)}) copy-start(bf16[8,16,16,64]{3,2,1,0:T(8,128)(2,1)S(1)} %broadcast_multiply_fusion.1) | copy-start | bytes 786436
  10.6 37.2 %collective-permute-start.3 = (bf16[1,16384]{1,0:T(2,128)(2,1)}, bf16[1,16384]{1,0:T(2,128)(2,1)S(1)}, u32[]{:S(2)}, u32[]{:S(2)}) collective-permute-start(bf16[1,16384]{1,0:T(2,128)(2,1)} %reshape.524), channel_id=1, source_target_pairs={} | collective-permute-start | bytes 98312 | tf_op jit(solution)/shard_map/ppermute | solution.py:16
  11.3 36.1 %collective-permute-start.4 = (bf16[8,1024]{1,0:T(8,128)(2,1)S(1)}, bf16[8,1024]{1,0:T(8,128)(2,1)S(1)}, u32[]{:S(2)}, u32[]{:S(2)}) collective-permute-start(bf16[8,1024]{1,0:T(8,128)(2,1)S(1)} %reshape.526), channel_id=1, source_target_pairs={{0,16},{8,24},{1,17},{9,25},{2,18},{10,26},{3,19},{11,27},{4,20},{... | collective-permute-start | bytes 49160 | tf_op jit(solution)/shard_map/ppermute | solution.py:16
  17.6 29.9 %collective-permute-start.5 = (bf16[8,1024]{1,0:T(8,128)(2,1)S(1)}, bf16[8,1024]{1,0:T(8,128)(2,1)S(1)}, u32[]{:S(2)}, u32[]{:S(2)}) collective-permute-start(bf16[8,1024]{1,0:T(8,128)(2,1)S(1)} %reshape.528), channel_id=1, source_target_pairs={{0,8},{8,16},{16,24},{1,9},{9,17},{17,25},{2,10},{10,18},{18,26},{... | collective-permute-start | bytes 49160 | tf_op jit(solution)/shard_map/ppermute | solution.py:16
  21.2 24.8 %collective-permute-start.6 = (bf16[1,1024]{1,0:T(2,128)(2,1)S(1)}, bf16[1,1024]{1,0:T(2,128)(2,1)S(1)}, u32[]{:S(2)}, u32[]{:S(2)}) collective-permute-start(bf16[1,1024]{1,0:T(2,128)(2,1)S(1)} %reshape.530), channel_id=1, source_target_pairs={} | collective-permute-start | bytes 6152 | tf_op jit(solution)/shard_map/ppermute | solution.py:16
  21.9 20.8 %collective-permute-start.9 = (bf16[1,64]{1,0:T(2,128)(2,1)S(1)}, bf16[1,64]{1,0:T(2,128)(2,1)S(1)}, u32[]{:S(2)}, u32[]{:S(2)}) collective-permute-start(bf16[1,64]{1,0:T(2,128)(2,1)S(1)} %slice_bitcast_fusion), channel_id=1, source_target_pairs={} | collective-permute-start | bytes 392 | tf_op jit(solution)/shard_map/ppermute | solution.py:16
  42.7 2.6 collective-permute-start.8
  45.3 2.0 collective-permute-start.7
  46.0 92.3 %collective-permute-start = (bf16[1,18496]{1,0:T(2,128)(2,1)}, bf16[1,18496]{1,0:T(2,128)(2,1)}, u32[]{:S(2)}, u32[]{:S(2)}) collective-permute-start(bf16[1,18496]{1,0:T(2,128)(2,1)} %convert_element_type.107), channel_id=1, source_target_pairs={} | collective-permute-start | bytes 110984 | tf_op jit(solution)/shard_map/ppermute | solution.py:16
  56.8 36.1 %copy-start.3 = (bf16[27,64,128]{2,1,0:T(8,128)(2,1)S(1)}, bf16[27,64,128]{2,1,0:T(8,128)(2,1)}, u32[]{:S(2)}) copy-start(bf16[27,64,128]{2,1,0:T(8,128)(2,1)} %param.30) | copy-start | bytes 1327108
  90.2 25.3 %copy-start.7 = (bf16[4,8,8,64]{3,2,1,0:T(8,128)(2,1)}, bf16[4,8,8,64]{3,2,1,0:T(8,128)(2,1)S(1)}, u32[]{:S(2)}) copy-start(bf16[4,8,8,64]{3,2,1,0:T(8,128)(2,1)S(1)} %slice.763) | copy-start | bytes 98308
  90.9 27.8 %copy-start.6 = (bf16[4,8,8,64]{3,2,1,0:T(8,128)(2,1)}, bf16[4,8,8,64]{3,2,1,0:T(8,128)(2,1)S(1)}, u32[]{:S(2)}) copy-start(bf16[4,8,8,64]{3,2,1,0:T(8,128)(2,1)S(1)} %slice.768) | copy-start | bytes 98308
  91.1 28.4 %copy-start.4 = (bf16[4,8,8,64]{3,2,1,0:T(8,128)(2,1)}, bf16[4,8,8,64]{3,2,1,0:T(8,128)(2,1)S(1)}, u32[]{:S(2)}) copy-start(bf16[4,8,8,64]{3,2,1,0:T(8,128)(2,1)S(1)} %slice.769) | copy-start | bytes 98308
  91.1 12.8 %copy-start.33 = (bf16[4,8,8,64]{3,2,1,0:T(8,128)(2,1)S(1)}, bf16[4,8,8,64]{3,2,1,0:T(8,128)(2,1)}, u32[]{:S(2)}) copy-start(bf16[4,8,8,64]{3,2,1,0:T(8,128)(2,1)} %slice.746) | copy-start | bytes 98308
  91.1 16.9 %copy-start.32 = (bf16[4,8,8,64]{3,2,1,0:T(8,128)(2,1)S(1)}, bf16[4,8,8,64]{3,2,1,0:T(8,128)(2,1)}, u32[]{:S(2)}) copy-start(bf16[4,8,8,64]{3,2,1,0:T(8,128)(2,1)} %slice.750) | copy-start | bytes 98308
  92.9 16.0 %copy-start.27 = (bf16[4,8,8,64]{3,2,1,0:T(8,128)(2,1)S(1)}, bf16[4,8,8,64]{3,2,1,0:T(8,128)(2,1)}, u32[]{:S(2)}) copy-start(bf16[4,8,8,64]{3,2,1,0:T(8,128)(2,1)} %slice.751) | copy-start | bytes 98308
  95.6 14.1 %copy-start.23 = (bf16[4,8,8,64]{3,2,1,0:T(8,128)(2,1)S(1)}, bf16[4,8,8,64]{3,2,1,0:T(8,128)(2,1)}, u32[]{:S(2)}) copy-start(bf16[4,8,8,64]{3,2,1,0:T(8,128)(2,1)} %slice.752) | copy-start | bytes 98308
  97.3 13.3 %copy-start.19 = (bf16[4,8,8,64]{3,2,1,0:T(8,128)(2,1)S(1)}, bf16[4,8,8,64]{3,2,1,0:T(8,128)(2,1)}, u32[]{:S(2)}) copy-start(bf16[4,8,8,64]{3,2,1,0:T(8,128)(2,1)} %slice.754) | copy-start | bytes 98308
  130.1 23.4 %copy-start.5 = (bf16[4,8,8,64]{3,2,1,0:T(8,128)(2,1)S(1)}, bf16[4,8,8,64]{3,2,1,0:T(8,128)(2,1)}, u32[]{:S(2)}) copy-start(bf16[4,8,8,64]{3,2,1,0:T(8,128)(2,1)} %copy-done.4) | copy-start | bytes 98308
  130.6 31.5 %copy-start = (f32[8,16,16,64]{3,2,1,0:T(8,128)S(1)}, f32[8,16,16,64]{3,2,1,0:T(8,128)}, u32[]{:S(2)}) copy-start(f32[8,16,16,64]{3,2,1,0:T(8,128)} %reshape.539) | copy-start | bytes 1572868
  142.7 6.5 %collective-permute-start.1 = (bf16[8,1088]{1,0:T(8,128)(2,1)S(1)}, bf16[8,1088]{1,0:T(8,128)(2,1)S(1)}, u32[]{:S(2)}, u32[]{:S(2)}) collective-permute-start(bf16[8,1088]{1,0:T(8,128)(2,1)S(1)} %convert_element_type.109), channel_id=1, source_target_pairs={{16,0},{24,8},{17,1},{25,9},{18,2},{26,10},{19,3},{27,11},{20,4},{... | collective-permute-start | bytes 52232 | tf_op jit(solution)/shard_map/ppermute | solution.py:16
  152.2 5.6 %collective-permute-start.2 = (bf16[8,1024]{1,0:T(8,128)(2,1)S(1)}, bf16[8,1024]{1,0:T(8,128)(2,1)S(1)}, u32[]{:S(2)}, u32[]{:S(2)}) collective-permute-start(bf16[8,1024]{1,0:T(8,128)(2,1)S(1)} %convert_element_type.111), channel_id=1, source_target_pairs={{8,0},{16,8},{24,16},{9,1},{17,9},{25,17},{10,2},{18,10},{26,18},{... | collective-permute-start | bytes 49160 | tf_op jit(solution)/shard_map/ppermute | solution.py:16
  (22 other events, 230.7 us)
Sparse Core Ops, SparseCore 0:
  120.5 130.5 all-reduce.3
where the time goes:
time: 263 us; the launch traced here: 260 us
  waiting for transfers between devices  94.5 us (36%)
  local copies, waits for them, and re-layouts  65.6 us (25%)
  matrix products  55.9 us (21%)
  starting transfers between devices  17.2 us (7%)
  between operations  14.9 us (6%)
  other arithmetic  12.1 us (5%)
    psum x1, waiting for transfers between devices, body(): summed = lax.psum(grads, ('brick', 'batch'))  86.2 us
    slice x30, local copies, waits for them, and re-layouts, pick(): return lax.slice_in_dim(field, tap, tap + 2 * count - 1, 2, axis)  40.5 us
    dot_general x27, matrix products, adjoint(): jnp.einsum('abco,abci->oi', chosen, masked, preferred_element_type=jnp.fl...  28.1 us
    dot_general x27, matrix products, adjoint(): jnp.einsum('abco,oi->abci', chosen, weight[index], preferred_element_type...  20.8 us
    ppermute x10, starting transfers between devices, from_behind(): return lax.ppermute(shard, axis, pairs)  17.2 us
    ppermute x10, waiting for transfers between devices, from_behind(): return lax.ppermute(shard, axis, pairs)  8.22 us
    dot_general x27, matrix products, spread(): jnp.einsum('abci,oi->abco', window, weight[9 * tap_x + 3 * tap_y + tap_z]...  7.06 us
  transfers between devices with their start and end apart: 11, of which 4 were waited for; matrix products, arithmetic and copies ran while one was open for 49% of the time, Pallas kernels for 0%

commit v1 on v0

--- a/solution.py
+++ b/solution.py
@@ -147,7 +147,8 @@
     coarse_grad = (
         (back * coarse_keep.astype(jnp.float32)).astype(jnp.bfloat16).reshape(coarse.shape)
     )
-    summed = lax.psum(grads, ("brick", "batch"))
+    blocks = lax.all_gather(grads, ("brick", "batch"), axis=0, tiled=False)
+    summed = blocks.sum(axis=0)
     scale = 1.0 / math.sqrt(
         lax.axis_size("brick") * lax.axis_size("batch") * size_x * size_y * size_z
     )

time: 263 us -> 233 us (0.89)
  local copies, waits for them, and re-layouts: 65.6 us -> 26.9 us
  waiting for transfers between devices: 94.5 us -> 126 us
  matrix products: 55.9 us -> 26 us
  other arithmetic: 12.1 us -> 20.3 us
    all_gather x0 -> x1, waiting for transfers between devices: none -> 117 us  [body(): blocks = lax.all_gather(grads, ('brick', 'batch'), axis=0, tiled=False)]
    psum x1 -> x0, waiting for transfers between devices: 86.2 us -> none  [body(): summed = lax.psum(grads, ('brick', 'batch'))]
    slice x30, local copies, waits for them, and re-layouts: 40.5 us -> 5.18 us  [pick(): return lax.slice_in_dim(field, tap, tap + 2 * count - 1, 2, axis)]
    dot_general x27, matrix products: 28.1 us -> 5.29 us  [adjoint(): jnp.einsum('abco,abci->oi', chosen, masked, preferred_element_type=jnp.fl...]
    reduce_sum x0 -> x1, other arithmetic: none -> 10.2 us  [body(): summed = blocks.sum(axis=0)]
    dot_general x27, matrix products: 20.8 us -> 14.3 us  [adjoint(): jnp.einsum('abco,oi->abci', chosen, weight[index], preferred_element_type...]
  transfers between devices with their start and end apart: 11 -> 11, of which waited for: 4 -> 4; matrix products, arithmetic and copies ran while one was open for 49% -> 19% of each run, Pallas kernels for 0% -> 0%
where the time goes in v1:
time: 233 us; the launch traced here: 232 us
  waiting for transfers between devices  126 us (54%)
  local copies, waits for them, and re-layouts  26.9 us (12%)
  matrix products  26 us (11%)
  other arithmetic  20.3 us (9%)
  starting transfers between devices  17.2 us (7%)
  between operations  15.7 us (7%)
    all_gather x1, waiting for transfers between devices, body(): blocks = lax.all_gather(grads, ('brick', 'batch'), axis=0, tiled=False)  117 us
    ppermute x10, starting transfers between devices, from_behind(): return lax.ppermute(shard, axis, pairs)  17.2 us
    dot_general x27, matrix products, adjoint(): jnp.einsum('abco,oi->abci', chosen, weight[index], preferred_element_type...  14.3 us
    reduce_sum x1, other arithmetic, body(): summed = blocks.sum(axis=0)  10.2 us
    ppermute x10, waiting for transfers between devices, from_behind(): return lax.ppermute(shard, axis, pairs)  8.41 us
    dot_general x27, matrix products, spread(): jnp.einsum('abci,oi->abco', window, weight[9 * tap_x + 3 * tap_y + tap_z]...  6.35 us
    dot_general x27, matrix products, adjoint(): jnp.einsum('abco,abci->oi', chosen, masked, preferred_element_type=jnp.fl...  5.29 us
    slice x30, local copies, waits for them, and re-layouts, pick(): return lax.slice_in_dim(field, tap, tap + 2 * count - 1, 2, axis)  5.18 us
  transfers between devices with their start and end apart: 11, of which 4 were waited for; matrix products, arithmetic and copies ran while one was open for 19% of the time, Pallas kernels for 0%

profile of v1, /device:TPU:0, one launch (start us, length us, event | category | flops | bytes accessed | tf_op | source)
XLA Modules:
  0.0 231.7 jit_solution(2063388781603478803)
XLA Ops:
  7.2 1.3 reshape.523
  10.6 5.9 %collective-permute-start.4 = (bf16[8,1024]{1,0:T(8,128)(2,1)S(1)}, bf16[8,1024]{1,0:T(8,128)(2,1)S(1)}, u32[]{:S(2)}, u32[]{:S(2)}) collective-permute-start(bf16[8,1024]{1,0:T(8,128)(2,1)S(1)} %reshape.526), channel_id=1, source_target_pairs={{0,16},{8,24},{1,17},{9,25},{2,18},{10,26},{3,19},{11,27},{4,20},{... | collective-permute-start | bytes 49160 | tf_op jit(solution)/shard_map/ppermute | solution.py:16
  16.9 3.5 %collective-permute-start.5 = (bf16[8,1024]{1,0:T(8,128)(2,1)S(1)}, bf16[8,1024]{1,0:T(8,128)(2,1)S(1)}, u32[]{:S(2)}, u32[]{:S(2)}) collective-permute-start(bf16[8,1024]{1,0:T(8,128)(2,1)S(1)} %reshape.528), channel_id=1, source_target_pairs={{0,8},{8,16},{16,24},{1,9},{9,17},{17,25},{2,10},{10,18},{18,26},{... | collective-permute-start | bytes 49160 | tf_op jit(solution)/shard_map/ppermute | solution.py:16
  23.2 1.3 collective-permute-start.8
  24.5 1.3 collective-permute-done.8
  27.7 1.4 scatter.26
  48.6 2.1 copy.88
  50.7 2.5 %reshape.518 = f32[10,18,18,64]{3,2,1,0:T(8,128)S(1)} reshape(f32[5,2,9,2,9,2,64]{6,5,4,3,2,1,0:T(2,128)} %bitcast.610) | data formatting | bytes 1658880 | tf_op jit(solution)/shard_map/reshape | solution.py:49
  54.0 1.3 collective-permute-start
  55.3 1.5 slice.770
  70.9 1.1 fusion.48
  73.8 1.3 collective-permute-start.1
  75.1 1.1 convolution_add_fusion.20
  76.2 4.1 %collective-permute-done.1 = bf16[8,1088]{1,0:T(8,128)(2,1)S(1)} collective-permute-done((bf16[8,1088]{1,0:T(8,128)(2,1)S(1)}, bf16[8,1088]{1,0:T(8,128)(2,1)S(1)}, u32[]{:S(2)}, u32[]{:S(2)}) %collective-permute-start.1) | collective-permute-done | bytes 17440 | tf_op jit(solution)/shard_map/ppermute | solution.py:16
  80.5 1.6 fusion.47
  82.1 1.3 fusion.50
  83.4 1.3 collective-permute-start.2
  86.4 3.0 %collective-permute-done.2 = bf16[8,1024]{1,0:T(8,128)(2,1)S(1)} collective-permute-done((bf16[8,1024]{1,0:T(8,128)(2,1)S(1)}, bf16[8,1024]{1,0:T(8,128)(2,1)S(1)}, u32[]{:S(2)}, u32[]{:S(2)}) %collective-permute-start.2) | collective-permute-done | bytes 16416 | tf_op jit(solution)/shard_map/ppermute | solution.py:16
  89.5 1.1 slice_add_fusion.3
  90.6 3.0 %scatter-add.14 = f32[9,17,17,64]{3,2,1,0:T(8,128)} dynamic-update-slice(f32[9,17,17,64]{3,2,1,0:T(8,128)} %fusion.47, f32[8,16,1,64]{3,2,1,0:T(1,128)S(1)} %slice_add_fusion.3, s32[]{:T(128)} %constant.355.clone.1, s32[]{:T(128)} %constant.355.clone.1, s32[]{:T(128)} %constant.361.clone.1, s32[]{:T(128)} %constant.356.clone.1) | dynamic-update-slice | bytes 65540 | tf_op jit(solution)/shard_map/scatter-add | solution.py:128
  93.6 1.7 fusion.45
  95.4 1.1 reshape.522
  96.4 117.3 %all-gather.3.cloned.1.call-done = f32[864,64,128]{2,1,0:T(8,128)} async-done(((f32[27,64,128]{2,1,0:T(8,128)}), f32[864,64,128]{2,1,0:T(8,128)}) %all-gather.3.cloned.1.call-update) | async-done | bytes 28311568 | tf_op jit(solution)/shard_map/all_gather | solution.py:150
  213.7 10.2 %reduce_sum.9 = f32[27,64,128]{2,1,0:T(8,128)S(1)} reduce(f32[32,27,64,128]{3,2,1,0:T(8,128)} %bitcast.609, f32[]{:T(128)} %constant.359.clone.1), dimensions={0}, to_apply=%region_0.1 | reduce | flops 6856704 | bytes 29196292 | tf_op jit(solution)/shard_map/reduce_sum | solution.py:151
  (277 shorter events, 44.8 us)
Async XLA Ops:
  7.2 15.9 %copy-start.47 = (bf16[1,1,4,8,1024]{4,3,2,1,0:T(8,128)(2,1)S(1)}, bf16[1,1,4,8,1024]{4,3,2,1,0:T(8,128)(2,1)}, u32[]{:S(2)}) copy-start(bf16[1,1,4,8,1024]{4,3,2,1,0:T(8,128)(2,1)} %param.26) | copy-start | bytes 196612
  7.2 206.5 %all-gather.3.cloned.1.call-start = ((), (), s32[]{:S(2)}) async-start(), calls=%async_computation | async-start | bytes 29196288 | tf_op jit(solution)/shard_map/all_gather | solution.py:150
  9.8 17.1 %collective-permute-start.3 = (bf16[1,16384]{1,0:T(2,128)(2,1)S(1)}, bf16[1,16384]{1,0:T(2,128)(2,1)S(1)}, u32[]{:S(2)}, u32[]{:S(2)}) collective-permute-start(bf16[1,16384]{1,0:T(2,128)(2,1)S(1)} %reshape.524), channel_id=1, source_target_pairs={} | collective-permute-start | bytes 98312 | tf_op jit(solution)/shard_map/ppermute | solution.py:16
  10.6 16.1 %collective-permute-start.4 = (bf16[8,1024]{1,0:T(8,128)(2,1)S(1)}, bf16[8,1024]{1,0:T(8,128)(2,1)S(1)}, u32[]{:S(2)}, u32[]{:S(2)}) collective-permute-start(bf16[8,1024]{1,0:T(8,128)(2,1)S(1)} %reshape.526), channel_id=1, source_target_pairs={{0,16},{8,24},{1,17},{9,25},{2,18},{10,26},{3,19},{11,27},{4,20},{... | collective-permute-start | bytes 49160 | tf_op jit(solution)/shard_map/ppermute | solution.py:16
  16.9 9.8 %collective-permute-start.5 = (bf16[8,1024]{1,0:T(8,128)(2,1)S(1)}, bf16[8,1024]{1,0:T(8,128)(2,1)S(1)}, u32[]{:S(2)}, u32[]{:S(2)}) collective-permute-start(bf16[8,1024]{1,0:T(8,128)(2,1)S(1)} %reshape.528), channel_id=1, source_target_pairs={{0,8},{8,16},{16,24},{1,9},{9,17},{17,25},{2,10},{10,18},{18,26},{... | collective-permute-start | bytes 49160 | tf_op jit(solution)/shard_map/ppermute | solution.py:16
  20.5 6.0 %collective-permute-start.6 = (bf16[1,1024]{1,0:T(2,128)(2,1)S(1)}, bf16[1,1024]{1,0:T(2,128)(2,1)S(1)}, u32[]{:S(2)}, u32[]{:S(2)}) collective-permute-start(bf16[1,1024]{1,0:T(2,128)(2,1)S(1)} %reshape.530), channel_id=1, source_target_pairs={} | collective-permute-start | bytes 6152 | tf_op jit(solution)/shard_map/ppermute | solution.py:16
  21.1 2.0 collective-permute-start.9
  23.2 2.6 %collective-permute-start.8 = (bf16[8,64]{1,0:T(8,128)(2,1)S(1)}, bf16[8,64]{1,0:T(8,128)(2,1)S(1)}, u32[]{:S(2)}, u32[]{:S(2)}) collective-permute-start(bf16[8,64]{1,0:T(8,128)(2,1)S(1)} %bitcast.614), channel_id=1, source_target_pairs={{0,24},{1,25},{2,26},{3,27},{4,28},{5,29},{6,30},{7,31}} | collective-permute-start | bytes 3080 | tf_op jit(solution)/shard_map/ppermute | solution.py:16
  25.8 0.7 collective-permute-start.7
  54.0 16.9 %collective-permute-start = (bf16[1,18496]{1,0:T(2,128)(2,1)}, bf16[1,18496]{1,0:T(2,128)(2,1)}, u32[]{:S(2)}, u32[]{:S(2)}) collective-permute-start(bf16[1,18496]{1,0:T(2,128)(2,1)} %convert_element_type.107), channel_id=1, source_target_pairs={} | collective-permute-start | bytes 110984 | tf_op jit(solution)/shard_map/ppermute | solution.py:16
  57.7 10.8 %copy-start.29 = (bf16[4,8,8,64]{3,2,1,0:T(8,128)(2,1)S(1)}, bf16[4,8,8,64]{3,2,1,0:T(8,128)(2,1)}, u32[]{:S(2)}) copy-start(bf16[4,8,8,64]{3,2,1,0:T(8,128)(2,1)} %copy-done.28) | copy-start | bytes 98308
  57.7 11.0 %copy-start.26 = (bf16[4,8,8,64]{3,2,1,0:T(8,128)(2,1)S(1)}, bf16[4,8,8,64]{3,2,1,0:T(8,128)(2,1)}, u32[]{:S(2)}) copy-start(bf16[4,8,8,64]{3,2,1,0:T(8,128)(2,1)} %copy-done.25) | copy-start | bytes 98308
  57.7 11.1 %copy-start.24 = (bf16[4,8,8,64]{3,2,1,0:T(8,128)(2,1)S(1)}, bf16[4,8,8,64]{3,2,1,0:T(8,128)(2,1)}, u32[]{:S(2)}) copy-start(bf16[4,8,8,64]{3,2,1,0:T(8,128)(2,1)} %copy-done.23) | copy-start | bytes 98308
  57.7 11.3 %copy-start.22 = (bf16[4,8,8,64]{3,2,1,0:T(8,128)(2,1)S(1)}, bf16[4,8,8,64]{3,2,1,0:T(8,128)(2,1)}, u32[]{:S(2)}) copy-start(bf16[4,8,8,64]{3,2,1,0:T(8,128)(2,1)} %copy-done.21) | copy-start | bytes 98308
  58.5 9.3 %copy-start.1 = (bf16[27,64,128]{2,1,0:T(8,128)(2,1)S(1)}, bf16[27,64,128]{2,1,0:T(8,128)(2,1)}, u32[]{:S(2)}) copy-start(bf16[27,64,128]{2,1,0:T(8,128)(2,1)} %param.30) | copy-start | bytes 1327108
  58.5 9.3 %copy-start.45 = (bf16[4,8,8,64]{3,2,1,0:T(8,128)(2,1)S(1)}, bf16[4,8,8,64]{3,2,1,0:T(8,128)(2,1)}, u32[]{:S(2)}) copy-start(bf16[4,8,8,64]{3,2,1,0:T(8,128)(2,1)} %copy-done.44) | copy-start | bytes 98308
  58.5 9.4 %copy-start.41 = (bf16[4,8,8,64]{3,2,1,0:T(8,128)(2,1)S(1)}, bf16[4,8,8,64]{3,2,1,0:T(8,128)(2,1)}, u32[]{:S(2)}) copy-start(bf16[4,8,8,64]{3,2,1,0:T(8,128)(2,1)} %copy-done.40) | copy-start | bytes 98308
  58.5 9.6 %copy-start.38 = (bf16[4,8,8,64]{3,2,1,0:T(8,128)(2,1)S(1)}, bf16[4,8,8,64]{3,2,1,0:T(8,128)(2,1)}, u32[]{:S(2)}) copy-start(bf16[4,8,8,64]{3,2,1,0:T(8,128)(2,1)} %copy-done.37) | copy-start | bytes 98308
  58.5 9.7 %copy-start.36 = (bf16[4,8,8,64]{3,2,1,0:T(8,128)(2,1)S(1)}, bf16[4,8,8,64]{3,2,1,0:T(8,128)(2,1)}, u32[]{:S(2)}) copy-start(bf16[4,8,8,64]{3,2,1,0:T(8,128)(2,1)} %copy-done.35) | copy-start | bytes 98308
  58.5 9.9 %copy-start.32 = (bf16[4,8,8,64]{3,2,1,0:T(8,128)(2,1)S(1)}, bf16[4,8,8,64]{3,2,1,0:T(8,128)(2,1)}, u32[]{:S(2)}) copy-start(bf16[4,8,8,64]{3,2,1,0:T(8,128)(2,1)} %copy-done.31) | copy-start | bytes 98308
  59.6 9.6 %copy-start.20 = (bf16[4,8,8,64]{3,2,1,0:T(8,128)(2,1)S(1)}, bf16[4,8,8,64]{3,2,1,0:T(8,128)(2,1)}, u32[]{:S(2)}) copy-start(bf16[4,8,8,64]{3,2,1,0:T(8,128)(2,1)} %copy-done.19) | copy-start | bytes 98308
  60.6 8.7 %copy-start.18 = (bf16[4,8,8,64]{3,2,1,0:T(8,128)(2,1)S(1)}, bf16[4,8,8,64]{3,2,1,0:T(8,128)(2,1)}, u32[]{:S(2)}) copy-start(bf16[4,8,8,64]{3,2,1,0:T(8,128)(2,1)} %copy-done.17) | copy-start | bytes 98308
  73.8 6.5 %collective-permute-start.1 = (bf16[8,1088]{1,0:T(8,128)(2,1)S(1)}, bf16[8,1088]{1,0:T(8,128)(2,1)S(1)}, u32[]{:S(2)}, u32[]{:S(2)}) collective-permute-start(bf16[8,1088]{1,0:T(8,128)(2,1)S(1)} %convert_element_type.109), channel_id=1, source_target_pairs={{16,0},{24,8},{17,1},{25,9},{18,2},{26,10},{19,3},{27,11},{20,4},{... | collective-permute-start | bytes 52232 | tf_op jit(solution)/shard_map/ppermute | solution.py:16
  83.4 6.0 %collective-permute-start.2 = (bf16[8,1024]{1,0:T(8,128)(2,1)S(1)}, bf16[8,1024]{1,0:T(8,128)(2,1)S(1)}, u32[]{:S(2)}, u32[]{:S(2)}) collective-permute-start(bf16[8,1024]{1,0:T(8,128)(2,1)S(1)} %convert_element_type.111), channel_id=1, source_target_pairs={{8,0},{16,8},{24,16},{9,1},{17,9},{25,17},{10,2},{18,10},{26,18},{... | collective-permute-start | bytes 49160 | tf_op jit(solution)/shard_map/ppermute | solution.py:16
  (36 other events, 188.4 us)
Sparse Core Ops, SparseCore 0:
  42.2 171.4 all-gather.2
